TPU v7x, 512 devices: a whole 4x8x8 slice. The times are simulated.
512 devices in a mesh: rep: 32 (over x, z), tp: 16 (over y, core).
Axes of the slice: x: 4, y: 8, z: 8, core: 2. Of those that a mesh axis runs over, the one named last changes fastest.
Arguments:
- queries: bfloat16 [10240, 8192], P('rep', 'tp'), may hold values from -30 to 30
- fresh_kv: bfloat16 [10240, 4096], P('rep', 'tp'), may hold values from -6 to 6, as said below
- kv_cache: bfloat16 [1408, 16, 8, 256], P('rep', 'tp'), may hold values from -6 to 6, as said below
- cached_len: int32 [640], P('rep'), may hold values from 1 to 48, as said below
- page_table: int32 [640, 6], P('rep'), may hold values from 0 to 43, as said below
- out_weight: bfloat16 [8192, 4096], P('tp'), may hold values from -0.09375 to 0.09375
- adapter_down: bfloat16 [64, 64, 8192], P('rep', None, 'tp'), may hold values from -0.0625 to 0.0625
- pooled_up_weight: bfloat16 [64, 64, 4096], P('rep', None, 'tp'), may hold values from -0.75 to 0.75
- adapter_ids: int32 [640], P('rep'), may hold values from 0 to 63, as said below
- pool_slot: int32 [64], replicated, may hold values from 0 to 63, as said below
Outputs:
- adapted_output: bfloat16 [10240, 4096], P('rep', 'tp')
Inputs may be any that keep to these rules, and one draw needn't show every extreme that they name: `kv_cache`: slots that hold the same key-value head are equal. `fresh_kv`: slots that hold the same key-value head are equal. `cached_len`: A row with cached length n uses its first ceil(n / 8) page table entries; in every replica some row has 48. `page_table`: entries index the 44 pages of the row's own replica. The pages that a row uses are distinct, no page is used by two rows of one replica, every page of a replica is used, and entries past a row's used pages repeat its first page. `adapter_ids`: row r of replica i is entry i * 20 + r. The owner of adapter a is replica pool_slot[a] // 2. Within one replica at most 2 rows name adapters of one owner, and one owner, the same for all replicas, is named by exactly 2 rows of every replica. A permutation: adapter a's blocks are adapter_down[pool_slot[a]] and pooled_up_weight[pool_slot[a]].
All inputs are finite; a program needn't handle non-finite values.
Results may differ from a plain program's by a relative error of at most 0.023.
Values may be sent and summed in bfloat16 or wider, within the bound.
No kernel may reach another device: no remote copies, remote signals or barrier semaphores. Data moves between devices by JAX's collectives and lax.ppermute only.
A program may use at most 64 MiB of HBM per device.

v0:
```python
import math
import jax
import jax.numpy as jnp
from jax import lax
from jax.sharding import PartitionSpec as P

ADAPTER_SCALE = 2.0


def shards(
    queries,
    fresh_kv,
    kv_cache,
    cached_len,
    page_table,
    out_weight,
    adapter_down,
    pooled_up_weight,
    adapter_ids,
    pool_slot,
):
    row_count = cached_len.shape[0]
    token_count = queries.shape[0]
    per_row = token_count // row_count
    slot_count = kv_cache.shape[1]
    page_len = kv_cache.shape[2]
    head_dim = kv_cache.shape[3] // 2
    feat_width = queries.shape[1]
    head_count = feat_width // head_dim
    heads_per_slot = head_count // slot_count
    cache_span = page_table.shape[1] * page_len
    output_columns = pooled_up_weight.shape[2]
    paged_kv = (
        kv_cache[page_table]
        .transpose(0, 2, 1, 3, 4)
        .reshape(row_count, slot_count, cache_span, 2 * head_dim)
    )
    recent = fresh_kv.reshape(row_count, per_row, slot_count, 2 * head_dim).transpose(0, 2, 1, 3)
    entries = jnp.concatenate([paged_kv, recent], axis=2)
    key_part = entries[..., :head_dim]
    value_part = entries[..., head_dim:]
    query_rows = queries.reshape(
        row_count, per_row, slot_count, heads_per_slot, head_dim
    ).transpose(0, 2, 1, 3, 4)
    query_rows = query_rows.reshape(row_count, slot_count, per_row * heads_per_slot, head_dim)
    scores = jnp.einsum(
        "rsad,rskd->rsak", query_rows, key_part, preferred_element_type=jnp.float32
    ) / math.sqrt(head_dim)
    entry_ids = jnp.arange(cache_span + per_row)[None, None, None, :]
    token_ids = (jnp.arange(per_row * heads_per_slot) // heads_per_slot)[None, None, :, None]
    allowed = jnp.where(
        entry_ids < cache_span,
        entry_ids < cached_len[:, None, None, None],
        entry_ids - cache_span <= token_ids,
    )
    scores = jnp.where(allowed, scores, -jnp.inf)
    peak_score = jnp.max(scores, axis=-1, keepdims=True)
    raised = jnp.exp(scores - peak_score)
    weights = (raised / jnp.sum(raised, axis=-1, keepdims=True)).astype(jnp.bfloat16)
    attended = jnp.einsum(
        "rsak,rskd->rsad", weights, value_part, preferred_element_type=jnp.float32
    ).astype(jnp.bfloat16)
    attended = attended.reshape(row_count, slot_count, per_row, heads_per_slot, head_dim).transpose(
        0, 2, 1, 3, 4
    )
    attended = attended.reshape(token_count, feat_width)
    plain_output = (
        lax.psum_scatter(
            lax.dot_general(
                out_weight, attended, (((0,), (1,)), ((), ())), preferred_element_type=jnp.float32
            ).astype(jnp.bfloat16),
            "tp",
            scatter_dimension=0,
            tiled=True,
        )
        .astype(jnp.float32)
        .T
    )
    slot_hits = adapter_ids[:, None] == jnp.arange(pool_slot.shape[0])[None, :]
    pool_position = jnp.sum(jnp.where(slot_hits, pool_slot[None, :], 0), axis=1)
    replicas = lax.axis_size("rep")
    local_count = adapter_down.shape[0]
    capacity = (row_count + replicas - 1) // replicas + 1
    owner_of = pool_position // local_count
    local_slot = pool_position % local_count
    same_owner = owner_of[:, None] == owner_of[None, :]
    earlier = jnp.arange(row_count)[None, :] < jnp.arange(row_count)[:, None]
    seat_of = jnp.sum(same_owner & earlier, axis=1)
    target = owner_of * capacity + seat_of
    placing = jnp.arange(replicas * capacity)[:, None] == target[None, :]
    placing_mat = placing.astype(jnp.bfloat16)
    by_row = attended.reshape(row_count, per_row, feat_width)
    send_rows = jnp.einsum(
        "sr,rqf->sqf", placing_mat, by_row, preferred_element_type=jnp.float32
    ).astype(jnp.bfloat16)
    seat_slot = jnp.sum(jnp.where(placing, local_slot[None, :], 0), axis=1).astype(jnp.bfloat16)
    marker = jnp.broadcast_to(seat_slot[:, None, None], (replicas * capacity, 1, feat_width))
    payload = jnp.concatenate([send_rows, marker], axis=1).reshape(
        replicas, capacity, per_row + 1, feat_width
    )
    arrived = lax.all_to_all(payload, "rep", split_axis=0, concat_axis=0, tiled=True)
    arrived = arrived.reshape(replicas * capacity, per_row + 1, feat_width)
    seat_rows = arrived[:, :per_row, :]
    wants_one = arrived[:, per_row, 0] > 0.5
    shrink_both = jnp.einsum(
        "sqf,jkf->jsqk", seat_rows, adapter_down, preferred_element_type=jnp.float32
    )
    shrink_part = jnp.where(wants_one[:, None, None], shrink_both[1], shrink_both[0])
    down_projected = lax.psum(shrink_part.astype(jnp.bfloat16), "tp")
    up_both = jnp.einsum(
        "sqk,jkd->jsqd", down_projected, pooled_up_weight, preferred_element_type=jnp.float32
    )
    seat_delta = jnp.where(wants_one[:, None, None], up_both[1], up_both[0]).astype(jnp.bfloat16)
    returned = lax.all_to_all(
        seat_delta.reshape(replicas, capacity, per_row, output_columns),
        "rep",
        split_axis=0,
        concat_axis=0,
        tiled=True,
    ).reshape(replicas * capacity, per_row, output_columns)
    adapter_correction = jnp.einsum(
        "sr,sqd->rqd", placing_mat, returned, preferred_element_type=jnp.float32
    )
    adapted_output = plain_output + ADAPTER_SCALE * adapter_correction.reshape(
        token_count, output_columns
    )
    return adapted_output.astype(jnp.bfloat16)


def solution(mesh):
    return jax.shard_map(
        shards,
        mesh=mesh,
        in_specs=(
            P("rep", "tp"),
            P("rep", "tp"),
            P("rep", "tp", None, None),
            P("rep"),
            P("rep", None),
            P("tp", None),
            P("rep", None, "tp"),
            P("rep", None, "tp"),
            P("rep"),
            P(),
        ),
        out_specs=P("rep", "tp"),
        check_vma=False,
    )
```

profile of v0, /device:TPU:25, one launch (start us, length us, event | category | flops | bytes accessed | tf_op | source)
XLA Modules:
  0.0 249.2 jit_solution(3435918056866313754)
XLA Ops:
  6.5 0.8 iota_compare_fusion.3
  7.3 0.7 compare_select_fusion
  8.2 1.2 reshape.194
  9.5 0.7 gather_fusion
  10.2 0.4 fusion.37
  10.6 0.3 fusion.5
  10.9 0.3 copy-done.4
  11.8 0.3 convolution_convert_fusion.2
  12.3 0.6 convolution_convert_fusion.1
  13.1 0.5 reshape.196
  13.5 1.8 copy.36
  15.3 12.9 %all-to-all-start = ((bf16[32,2,17,512]{3,1,2,0:T(2,128)(2,1)}), bf16[32,2,17,512]{3,1,2,0:T(2,128)(2,1)S(1)}, u32[]{:S(2)}, u32[]{:S(2)}) async-start(bf16[32,2,17,512]{3,1,2,0:T(2,128)(2,1)} %copy.36), calls=%async_computation.1 | async-start | bytes 2228224 | tf_op jit(solution)/shard_map/all_to_all | solution.py:101
  28.5 26.2 %all-to-all-done = bf16[32,2,17,512]{3,1,2,0:T(2,128)(2,1)S(1)} async-done(((bf16[32,2,17,512]{3,1,2,0:T(2,128)(2,1)}), bf16[32,2,17,512]{3,1,2,0:T(2,128)(2,1)S(1)}, u32[]{:S(2)}, u32[]{:S(2)}) %all-to-all-start) | async-done | bytes 1114144 | tf_op jit(solution)/shard_map/all_to_all | solution.py:101
  54.7 0.3 copy.37
  55.0 1.2 compare_reduce_fusion
  56.2 0.4 convolution_bitcast_fusion.1
  56.7 0.9 fusion.7
  57.6 5.2 %fusion.1 = bf16[4096,320]{0,1:T(8,128)(2,1)} fusion(bf16[320,512]{1,0:T(8,128)(2,1)S(1)} %reshape_transpose_reshape.4, bf16[512,4096]{1,0:T(8,128)(2,1)} %param.15), kind=kOutput, calls=%fused_computation.3 | convolution fusion | flops 1343488000 | bytes 7143424 | tf_op jit(solution)/shard_map/dot_general | solution.py:69
  63.0 110.7 %all-reduce.2.cloned.1.call-done = bf16[64,16,64]{2,1,0:T(8,128)(2,1)} async-done(((bf16[64,16,64]{2,1,0:T(8,128)(2,1)}), bf16[64,16,64]{2,1,0:T(8,128)(2,1)}) %all-reduce.2.cloned.1.call-update) | async-done | bytes 131088 | tf_op jit(solution)/shard_map/psum | solution.py:109
  173.7 1.4 convolution_bitcast_fusion
  175.3 26.2 %all_to_all.10 = bf16[32,2,16,256]{3,2,1,0:T(8,128)(2,1)S(1)} all-to-all(bf16[32,2,16,256]{3,2,1,0:T(8,128)(2,1)S(1)} %select_convert_fusion), channel_id=1, replica_groups=mesh['rep'=32,'tp'=16] {'rep'}, dimensions={0} | all-to-all | bytes 1048576 | tf_op jit(solution)/shard_map/all_to_all | solution.py:114
  201.4 0.3 convolution_multiply_fusion.1
  201.8 38.9 %reduce-scatter.2.cloned.1.call-done = bf16[256,320]{0,1:T(8,128)(2,1)} async-done(((bf16[4096,320]{0,1:T(8,128)(2,1)}), bf16[256,320]{0,1:T(8,128)(2,1)}) %reduce-scatter.2.cloned.1.call-update) | async-done | bytes 163856 | tf_op jit(solution)/shard_map/reduce_scatter | solution.py:68
  240.7 1.6 fusion.16
  (35 shorter events, 1.9 us)
Async XLA Ops:
  6.5 2.9 %copy-start = (bf16[44,1,8,256]{3,2,1,0:T(8,128)(2,1)S(1)}, bf16[44,1,8,256]{3,2,1,0:T(8,128)(2,1)}, u32[]{:S(2)}) copy-start(bf16[44,1,8,256]{3,2,1,0:T(8,128)(2,1)} %param.12) | copy-start | bytes 540676
  6.5 3.6 %copy-start.2 = (bf16[320,256]{1,0:T(8,128)(2,1)S(1)}, bf16[320,256]{1,0:T(8,128)(2,1)}, u32[]{:S(2)}) copy-start(bf16[320,256]{1,0:T(8,128)(2,1)} %param.11) | copy-start | bytes 491524
  10.6 0.7 copy-start.4
  10.6 0.7 copy-start.5
  15.3 39.4 %all-to-all-start = ((bf16[32,2,17,512]{3,1,2,0:T(2,128)(2,1)}), bf16[32,2,17,512]{3,1,2,0:T(2,128)(2,1)S(1)}, u32[]{:S(2)}, u32[]{:S(2)}) async-start(bf16[32,2,17,512]{3,1,2,0:T(2,128)(2,1)} %copy.36), calls=%async_computation.1 | async-start | bytes 2228224 | tf_op jit(solution)/shard_map/all_to_all | solution.py:101
  28.2 28.0 %copy-start.3 = (bf16[2,64,512]{2,1,0:T(8,128)(2,1)S(1)}, bf16[2,64,512]{2,1,0:T(8,128)(2,1)}, u32[]{:S(2)}) copy-start(bf16[2,64,512]{2,1,0:T(8,128)(2,1)} %param.16) | copy-start | bytes 393220
  28.2 145.5 %all-reduce.2.cloned.1.call-start = ((), (), s32[]{:S(2)}) async-start(), calls=%async_computation.4 | async-start | bytes 524288 | tf_op jit(solution)/shard_map/psum | solution.py:109
  57.6 183.1 %reduce-scatter.2.cloned.1.call-start = ((), (), s32[]{:S(2)}) async-start(), calls=%async_computation.3 | async-start | bytes 2785280 | tf_op jit(solution)/shard_map/reduce_scatter | solution.py:68
  62.8 110.8 %copy-start.1 = (bf16[2,64,256]{2,1,0:T(8,128)(2,1)S(1)}, bf16[2,64,256]{2,1,0:T(8,128)(2,1)}, u32[]{:S(2)}) copy-start(bf16[2,64,256]{2,1,0:T(8,128)(2,1)} %param.17) | copy-start | bytes 196612
Sparse Core Ops, SparseCore 0:
  57.7 115.9 all-reduce.1
  176.5 64.1 reduce-scatter.1
where the time goes:
time: 250 us; the launch traced here: 249 us
  waiting for transfers between devices  176 us (70%)
  blocking collectives  26.2 us (10%)
  between operations  13.6 us (5%)
  starting transfers between devices  13 us (5%)
  matrix products  8.95 us (4%)
  other arithmetic  5.98 us (2%)
  local copies, waits for them, and re-layouts  5.7 us (2%)
    psum x1, waiting for transfers between devices, shards(): down_projected = lax.psum(shrink_part.astype(jnp.bfloat16), 'tp')  111 us
    reduce_scatter x1, waiting for transfers between devices, shards(): lax.psum_scatter(lax.dot_general(out_weight, attended, (((0,), (1,)), (()...  38.9 us
    all_to_all x1, waiting for transfers between devices, shards(): lax.all_to_all(payload, 'rep', split_axis=0, concat_axis=0, tiled=True)  26.2 us
    all_to_all x1, blocking collectives, shards(): lax.all_to_all(seat_delta.reshape(replicas, capacity, per_row, output_col...  26.2 us
    all_to_all x1, starting transfers between devices, shards(): lax.all_to_all(payload, 'rep', split_axis=0, concat_axis=0, tiled=True)  12.9 us
    dot_general x1, matrix products, shards(): lax.dot_general(out_weight, attended, (((0,), (1,)), ((), ())), preferred...  5.22 us
  transfers between devices with their start and end apart: 3, of which 3 were waited for; matrix products, arithmetic and copies ran while one was open for 3% of the time, Pallas kernels for 0%

commit v1 on v0

--- a/solution.py
+++ b/solution.py
@@ -106,7 +106,7 @@
         "sqf,jkf->jsqk", seat_rows, adapter_down, preferred_element_type=jnp.float32
     )
     shrink_part = jnp.where(wants_one[:, None, None], shrink_both[1], shrink_both[0])
-    down_projected = lax.psum(shrink_part.astype(jnp.bfloat16), "tp")
+    down_projected = jnp.sum(lax.all_gather(shrink_part.astype(jnp.bfloat16), "tp"), axis=0)
     up_both = jnp.einsum(
         "sqk,jkd->jsqd", down_projected, pooled_up_weight, preferred_element_type=jnp.float32
     )

time: 250 us -> 183 us (0.73)
  the two profiles are of different devices: /device:TPU:25 before, /device:TPU:27 now
where the time goes in v1:
time: 183 us; the launch traced here: 182 us
  waiting for transfers between devices  80.6 us (44%)
  blocking collectives  66.1 us (36%)
  between operations  13.6 us (7%)
  other arithmetic  9.19 us (5%)
  matrix products  8.04 us (4%)
  local copies, waits for them, and re-layouts  4.7 us (3%)
    all_to_all x1, blocking collectives, shards(): lax.all_to_all(payload, 'rep', split_axis=0, concat_axis=0, tiled=True)  42.4 us
    all_gather x1, waiting for transfers between devices, shards(): lax.all_gather(shrink_part.astype(jnp.bfloat16), 'tp')  42 us
    reduce_scatter x1, waiting for transfers between devices, shards(): lax.psum_scatter(lax.dot_general(out_weight, attended, (((0,), (1,)), (()...  38.5 us
    all_to_all x1, blocking collectives, shards(): lax.all_to_all(seat_delta.reshape(replicas, capacity, per_row, output_col...  23.7 us
    dot_general x1, matrix products, shards(): lax.dot_general(out_weight, attended, (((0,), (1,)), ((), ())), preferred...  5.25 us
  transfers between devices with their start and end apart: 2, of which 2 were waited for; matrix products, arithmetic and copies ran while one was open for 5% of the time, Pallas kernels for 0%

profile of v1, /device:TPU:27, one launch (start us, length us, event | category | flops | bytes accessed | tf_op | source)
XLA Modules:
  0.0 182.2 jit_solution(8570929437844157034)
XLA Ops:
  6.6 0.8 iota_compare_fusion.3
  7.3 0.7 compare_select_fusion
  8.2 1.2 reshape.194
  9.5 0.7 gather_fusion
  10.2 0.4 fusion.36
  10.6 0.3 fusion.5
  11.0 0.3 copy-done.4
  11.8 0.3 convolution_convert_fusion.2
  12.3 0.6 convolution_convert_fusion.1
  13.1 0.5 reshape.196
  13.6 0.8 copy.33
  14.3 42.4 %all_to_all.10 = bf16[32,2,17,512]{3,1,2,0:T(2,128)(2,1)S(1)} all-to-all(bf16[32,2,17,512]{3,1,2,0:T(2,128)(2,1)S(1)} %copy.33), channel_id=1, replica_groups=mesh['rep'=32,'tp'=16] {'rep'}, dimensions={0} | all-to-all | bytes 2228224 | tf_op jit(solution)/shard_map/all_to_all | solution.py:101
  56.7 0.3 copy.34
  57.0 1.2 compare_reduce_fusion
  58.3 0.5 convolution_bitcast_fusion.1
  58.7 0.9 fusion.6
  59.9 5.2 %fusion.1 = bf16[4096,320]{0,1:T(8,128)(2,1)} fusion(bf16[320,512]{1,0:T(8,128)(2,1)S(1)} %reshape_transpose_reshape.4, bf16[512,4096]{1,0:T(8,128)(2,1)} %param.15), kind=kOutput, calls=%fused_computation.3 | convolution fusion | flops 1343488000 | bytes 7143424 | tf_op jit(solution)/shard_map/dot_general | solution.py:69
  65.3 42.0 %all-gather.2.cloned.1.call-done = bf16[16,64,16,64]{3,2,0,1:T(8,128)(2,1)} async-done(((bf16[1,64,16,64]{3,2,0,1:T(8,128)(2,1)}), bf16[16,64,16,64]{3,2,0,1:T(8,128)(2,1)}) %all-gather.2.cloned.1.call-update) | async-done | bytes 2097168 | tf_op jit(solution)/shard_map/all_gather | solution.py:109
  107.3 3.2 %reduce_sum.52 = bf16[64,16,64]{2,1,0:T(8,128)(2,1)S(1)} reduce(bf16[16,64,16,64]{3,2,0,1:T(8,128)(2,1)} %all-gather.2.cloned.1.call-done, bf16[]{:T(256)} %constant.60.clone.1), dimensions={0}, to_apply=%region_6.7 | reduce | flops 983040 | bytes 2228226 | tf_op jit(solution)/shard_map/reduce_sum | solution.py:109
  110.5 0.4 convolution_bitcast_fusion
  111.1 23.7 %all_to_all.11 = bf16[32,2,16,256]{3,2,1,0:T(8,128)(2,1)S(1)} all-to-all(bf16[32,2,16,256]{3,2,1,0:T(8,128)(2,1)S(1)} %select_convert_fusion), channel_id=1, replica_groups=mesh['rep'=32,'tp'=16] {'rep'}, dimensions={0} | all-to-all | bytes 1048576 | tf_op jit(solution)/shard_map/all_to_all | solution.py:114
  134.8 0.3 convolution_multiply_fusion.1
  135.2 38.5 %reduce-scatter.2.cloned.1.call-done = bf16[256,320]{0,1:T(8,128)(2,1)} async-done(((bf16[4096,320]{0,1:T(8,128)(2,1)}), bf16[256,320]{0,1:T(8,128)(2,1)}) %reduce-scatter.2.cloned.1.call-update) | async-done | bytes 163856 | tf_op jit(solution)/shard_map/reduce_scatter | solution.py:68
  173.8 1.6 fusion.15
  (35 shorter events, 1.9 us)
Async XLA Ops:
  6.5 3.0 %copy-start = (bf16[44,1,8,256]{3,2,1,0:T(8,128)(2,1)S(1)}, bf16[44,1,8,256]{3,2,1,0:T(8,128)(2,1)}, u32[]{:S(2)}) copy-start(bf16[44,1,8,256]{3,2,1,0:T(8,128)(2,1)} %param.12) | copy-start | bytes 540676
  6.5 3.6 %copy-start.2 = (bf16[320,256]{1,0:T(8,128)(2,1)S(1)}, bf16[320,256]{1,0:T(8,128)(2,1)}, u32[]{:S(2)}) copy-start(bf16[320,256]{1,0:T(8,128)(2,1)} %param.11) | copy-start | bytes 491524
  6.5 100.7 %all-gather.2.cloned.1.call-start = ((), (), s32[]{:S(2)}) async-start(), calls=%async_computation.4 | async-start | bytes 4456448 | tf_op jit(solution)/shard_map/all_gather | solution.py:109
  10.6 0.7 copy-start.4
  10.6 0.7 copy-start.5
  56.7 1.6 copy-start.3
  59.6 114.2 %reduce-scatter.2.cloned.1.call-start = ((), (), s32[]{:S(2)}) async-start(), calls=%async_computation.3 | async-start | bytes 2785280 | tf_op jit(solution)/shard_map/reduce_scatter | solution.py:68
  65.3 45.2 %copy-start.1 = (bf16[2,64,256]{2,1,0:T(8,128)(2,1)S(1)}, bf16[2,64,256]{2,1,0:T(8,128)(2,1)}, u32[]{:S(2)}) copy-start(bf16[2,64,256]{2,1,0:T(8,128)(2,1)} %param.17) | copy-start | bytes 196612
Sparse Core Ops, SparseCore 0:
  59.7 47.4 all-gather.1
  110.1 63.6 reduce-scatter.1
